TPU v7x, 256 devices: a whole 4x4x8 slice. The times are simulated.
256 devices in a mesh: dp: 32 (over y, z), mp: 8 (over x, core).
Axes of the slice: x: 4, y: 4, z: 8, core: 2. Of those that a mesh axis runs over, the one named last changes fastest.
Arguments:
- hidden: bfloat16 [512, 32, 1024], P(('dp', 'mp')), may hold values from -96 to 96, as said below
- query_weight: bfloat16 [1024, 1024], P('dp', 'mp'), may hold values from -0.1875 to 0.1875
- w_key: bfloat16 [1024, 1024], P('dp', 'mp'), may hold values from -0.1875 to 0.1875
- w_value: bfloat16 [1024, 1024], P('dp', 'mp'), may hold values from -0.1875 to 0.1875
- rel_table: bfloat16 [512, 1024], P('dp'), may hold values from -6 to 6
- rel_bucket: int32 [32, 32], replicated, may hold values from 0 to 511
- w_out: bfloat16 [1024, 1024], P('mp', 'dp'), may hold values from -0.1875 to 0.1875
- w_up: bfloat16 [1024, 4096], P('dp', 'mp'), may hold values from -0.1875 to 0.1875
- w_down: bfloat16 [4096, 1024], P('mp', 'dp'), may hold values from -0.09375 to 0.09375
- w_proj: bfloat16 [1024, 128], P(('dp', 'mp')), may hold values from -0.1875 to 0.1875
- pages: bfloat16 [8192, 128, 128], P('dp'), may hold values from -0.59765625 to 0.59765625
- page_len: int32 [8192], P('dp'), may hold values from 1 to 128
- slot_per_page: int32 [8192], replicated, may hold values from 0 to 8191, as said below
- candidates: int32 [512, 16, 4], P(('dp', 'mp')), may hold values from 0 to 8191, as said below
Outputs:
- query_vectors: bfloat16 [512, 32, 128], P(('dp', 'mp'))
- scores: float32 [512, 16], P(('dp', 'mp'))
Inputs may be any that keep to these rules, and one draw needn't show every extreme that they name: slot_per_page is a permutation of the slots; the page in slot s is held by index s // 256 of dp. `candidates`: among the 128 page ids of the 2 queries of one device (queries in aligned blocks of 2), at most 8 have slots held by any one index of dp, and in every such block some index of dp holds exactly 8 of them. `hidden`: token states are finite.
All inputs are finite; a program needn't handle non-finite values.
Results may differ from a plain program's by a relative error of at most 0.025.
Values may be sent and summed in bfloat16 or wider, within the bound.
No kernel may reach another device: no remote copies, remote signals or barrier semaphores. Data moves between devices by JAX's collectives and lax.ppermute only.
A program may use at most 64 MiB of HBM per device.

v0:
```python
import jax
import jax.numpy as jnp
from jax import lax
from jax.sharding import PartitionSpec as P

HD = 64


def layer_norm(value):
    mean = jnp.mean(value, axis=-1, keepdims=True)
    centered = value - mean
    var = jnp.mean(centered * centered, axis=-1, keepdims=True)
    return centered / jnp.sqrt(var + 1e-07)


def add_rows(left, piece):
    return jnp.dot(left, piece, preferred_element_type=jnp.float32)


def return_maxima(maxima):
    return lax.all_to_all(
        maxima.astype(jnp.bfloat16), "dp", split_axis=0, concat_axis=0, tiled=True
    ).astype(maxima.dtype)


def body(
    hidden,
    query_weight,
    w_key,
    w_value,
    rel_table,
    rel_bucket,
    w_out,
    w_up,
    w_down,
    w_proj,
    pages,
    page_len,
    slot_per_page,
    candidates,
):
    qry_dev, qlen, width = hidden.shape
    heads_local = query_weight.shape[1] // HD
    cols = query_weight.shape[1]
    tokens = lax.all_gather(hidden, "mp", axis=0, tiled=True)
    group = tokens.shape[0]
    flat = tokens.reshape(group * qlen, width)
    left_rel = lax.all_gather(rel_table, "dp", axis=0, tiled=True)
    pieces = (
        lax.all_gather(query_weight, "dp", axis=0, tiled=True),
        lax.all_gather(w_key, "dp", axis=0, tiled=True),
        lax.all_gather(w_value, "dp", axis=0, tiled=True),
    )
    qsum = add_rows(flat, pieces[0])
    ksum = add_rows(flat, pieces[1])
    vsum = add_rows(flat, pieces[2])
    qrsum = add_rows(left_rel, pieces[0])
    krsum = add_rows(left_rel, pieces[1])
    rel_q = qrsum.astype(jnp.bfloat16)
    rel_k = krsum.astype(jnp.bfloat16)
    nbuck = rel_q.shape[0]
    qx = qsum.astype(jnp.bfloat16).reshape(group, qlen, heads_local, HD)
    kx = ksum.astype(jnp.bfloat16).reshape(group, qlen, heads_local, HD)
    vx = vsum.astype(jnp.bfloat16).reshape(group, qlen, heads_local, HD)
    rel_q = rel_q.reshape(nbuck, heads_local, HD)
    rel_k = rel_k.reshape(nbuck, heads_local, HD)
    onehot = (rel_bucket[:, :, None] == jnp.arange(nbuck, dtype=jnp.int32)[None, None, :]).astype(
        jnp.float32
    )
    scale = 1.0 / jnp.sqrt(jnp.float32(3 * HD))
    content = jnp.einsum("qihd,qjhd->qhij", qx, kx, preferred_element_type=jnp.float32)
    along_axis_name = jnp.einsum("qihd,bhd->qhib", qx, rel_k, preferred_element_type=jnp.float32)
    c2p = jnp.einsum("qhib,ijb->qhij", along_axis_name, onehot, precision=lax.Precision.HIGHEST)
    back = jnp.einsum("qjhd,bhd->qhjb", kx, rel_q, preferred_element_type=jnp.float32)
    p2c = jnp.einsum("qhjb,jib->qhij", back, onehot, precision=lax.Precision.HIGHEST)
    logits = (content + c2p + p2c) * scale
    probs = jax.nn.softmax(logits, axis=-1).astype(jnp.bfloat16)
    context_rows = jnp.einsum("qhij,qjhd->qihd", probs, vx, preferred_element_type=jnp.float32)
    context_rows = context_rows.astype(jnp.bfloat16).reshape(group * qlen, cols)
    attn_terms = jnp.dot(
        context_rows,
        lax.all_gather(w_out, "dp", axis=1, tiled=True),
        preferred_element_type=jnp.float32,
    )
    attn = lax.psum_scatter(
        attn_terms.astype(jnp.bfloat16), "mp", scatter_dimension=0, tiled=True
    ).astype(jnp.float32)
    own = hidden.reshape(qry_dev * qlen, width).astype(jnp.float32)
    mid = layer_norm(own + attn).astype(jnp.bfloat16)
    mid_all = lax.all_gather(mid, "mp", axis=0, tiled=True)
    up = add_rows(mid_all, lax.all_gather(w_up, "dp", axis=0, tiled=True))
    inner = jax.nn.gelu(up, approximate=False).astype(jnp.bfloat16)
    down_terms = jnp.dot(
        inner, lax.all_gather(w_down, "dp", axis=1, tiled=True), preferred_element_type=jnp.float32
    )
    mlp = lax.psum_scatter(
        down_terms.astype(jnp.bfloat16), "mp", scatter_dimension=0, tiled=True
    ).astype(jnp.float32)
    state = layer_norm(mid.astype(jnp.float32) + mlp).astype(jnp.bfloat16)
    width_out = w_proj.shape[1]
    proj = add_rows(state, lax.all_gather(w_proj, ("dp", "mp"), axis=0, tiled=True))
    vectors = (proj / jnp.sqrt(jnp.sum(proj * proj, axis=-1, keepdims=True) + 1e-06)).astype(
        jnp.bfloat16
    )
    vectors = vectors.reshape(qry_dev, qlen, width_out)
    page_owners = lax.axis_size("dp")
    pg_dev = pages.shape[0]
    ptok = pages.shape[1]
    ncand, ppc = (candidates.shape[1], candidates.shape[2])
    req = qry_dev * ncand * ppc
    cap = 2 * req // page_owners
    slots = slot_per_page[candidates.reshape(req)]
    dest = slots // pg_dev
    local = slots % pg_dev
    query_of = jnp.arange(req, dtype=jnp.int32) // (ncand * ppc)
    member = (dest[:, None] == jnp.arange(page_owners, dtype=jnp.int32)[None, :]).astype(jnp.int32)
    place = jnp.sum((jnp.cumsum(member, axis=0) - 1) * member, axis=1)
    index = dest * cap + place
    codes = jnp.full((page_owners * cap,), -1, jnp.int32).at[index].set(query_of * pg_dev + local)
    codes = codes.reshape(page_owners, cap)
    token_positions = jnp.arange(ptok, dtype=jnp.int32)
    rows_out = (
        jnp.zeros((page_owners * cap, qlen, width_out), jnp.bfloat16)
        .at[index]
        .set(vectors[query_of])
    )
    rows_out = rows_out.reshape(page_owners, cap, qlen, width_out)
    where_local = lax.all_to_all(codes, "dp", split_axis=0, concat_axis=0, tiled=True) % pg_dev
    chosen = pages[where_local]
    lens = page_len[where_local]
    sim = jnp.einsum(
        "snie,snte->snit",
        lax.all_to_all(rows_out, "dp", split_axis=0, concat_axis=0, tiled=True),
        chosen,
        preferred_element_type=jnp.float32,
    )
    valid = token_positions[None, None, None, :] < lens[:, :, None, None]
    returned = return_maxima(jnp.max(jnp.where(valid, sim, -1e30), axis=-1))
    best = returned.reshape(page_owners * cap, qlen)[index]
    best = best.reshape(qry_dev, ncand, ppc, qlen)
    scores = jnp.sum(jnp.max(best, axis=2), axis=-1)
    return (vectors, scores)


def solution(mesh):
    in_specs = (
        P(("dp", "mp"), None, None),
        P("dp", "mp"),
        P("dp", "mp"),
        P("dp", "mp"),
        P("dp", None),
        P(),
        P("mp", "dp"),
        P("dp", "mp"),
        P("mp", "dp"),
        P(("dp", "mp"), None),
        P("dp", None, None),
        P("dp"),
        P(),
        P(("dp", "mp"), None, None),
    )
    out_specs = (P(("dp", "mp"), None, None), P(("dp", "mp"), None))
    return jax.shard_map(body, mesh=mesh, in_specs=in_specs, out_specs=out_specs, check_vma=False)
```

profile of v0, /device:TPU:1, one launch (start us, length us, event | category | flops | bytes accessed | tf_op | source)
XLA Modules:
  0.0 620.8 jit_solution(7747046523202727993)
XLA Ops:
  8.7 41.4 %all_gather.32 = bf16[1024,128]{1,0:T(8,128)(2,1)S(1)} all-gather(bf16[32,128]{1,0:T(8,128)(2,1)} %param.15), channel_id=1, replica_groups=mesh['dp'=32,'mp'=8] {'dp'}, dimensions={0}, use_global_device_ids=true | all-gather | bytes 270336 | tf_op jit(solution)/shard_map/all_gather | solution.py:50
  50.1 38.1 %all_gather.33 = bf16[1024,128]{1,0:T(8,128)(2,1)S(1)} all-gather(bf16[32,128]{1,0:T(8,128)(2,1)} %param.16), channel_id=1, replica_groups=mesh['dp'=32,'mp'=8] {'dp'}, dimensions={0}, use_global_device_ids=true | all-gather | bytes 270336 | tf_op jit(solution)/shard_map/all_gather | solution.py:51
  88.1 37.2 %all_gather.31 = bf16[1024,128]{1,0:T(8,128)(2,1)S(1)} all-gather(bf16[32,128]{1,0:T(8,128)(2,1)} %param.17), channel_id=1, replica_groups=mesh['dp'=32,'mp'=8] {'dp'}, dimensions={0}, use_global_device_ids=true | all-gather | bytes 270336 | tf_op jit(solution)/shard_map/all_gather | solution.py:52
  125.3 35.7 %all_gather.35 = bf16[128,1024]{0,1:T(8,128)(2,1)S(1)} all-gather(bf16[128,32]{0,1:T(8,128)(2,1)} %param.20), channel_id=1, replica_groups=mesh['dp'=32,'mp'=8] {'dp'}, dimensions={1}, use_global_device_ids=true | all-gather | bytes 270336 | tf_op jit(solution)/shard_map/all_gather | solution.py:82
  161.0 1.7 convolution_convert_fusion.6
  162.9 1.7 convolution_convert_fusion.5
  165.3 1.7 convolution_convert_fusion.4
  175.7 73.5 %reduce-scatter.3.cloned.1.call-done = bf16[64,1024]{1,0:T(8,128)(2,1)} async-done(((bf16[512,1024]{1,0:T(8,128)(2,1)}), bf16[64,1024]{1,0:T(8,128)(2,1)}) %reduce-scatter.3.cloned.1.call-update) | async-done | bytes 131088 | tf_op jit(solution)/shard_map/reduce_scatter | solution.py:85
  251.4 1.7 divide_convert_fusion.3
  253.4 70.8 %all-gather.13.cloned.1.call-done = bf16[1024,512]{1,0:T(8,128)(2,1)} async-done(((bf16[32,512]{1,0:T(8,128)(2,1)}), bf16[1024,512]{1,0:T(8,128)(2,1)}) %all-gather.13.cloned.1.call-update) | async-done | bytes 1048592 | tf_op jit(solution)/shard_map/all_gather | solution.py:91
  324.1 76.3 %all-gather.15.cloned.1.call-done = bf16[512,1024]{0,1:T(8,128)(2,1)} async-done(((bf16[512,32]{0,1:T(8,128)(2,1)}), bf16[512,1024]{0,1:T(8,128)(2,1)}) %all-gather.15.cloned.1.call-update) | async-done | bytes 1048592 | tf_op jit(solution)/shard_map/all_gather | solution.py:94
  400.4 30.5 %all-gather.11.cloned.1.call-done = bf16[512,1024]{1,0:T(8,128)(2,1)} async-done(((bf16[64,1024]{1,0:T(8,128)(2,1)}), bf16[512,1024]{1,0:T(8,128)(2,1)}) %all-gather.11.cloned.1.call-update) | async-done | bytes 1048592 | tf_op jit(solution)/shard_map/all_gather | solution.py:90
  430.9 6.2 %convolution_convert_fusion.1 = bf16[512,1024]{1,0:T(8,128)(2,1)} fusion(bf16[512,1024]{0,1:T(8,128)(2,1)} %all-gather.15.cloned.1.call-done, bf16[512,1024]{1,0:T(8,128)(2,1)} %all-gather.11.cloned.1.call-done, bf16[1024,512]{1,0:T(8,128)(2,1)} %all-gather.13.cloned.1.call-done), kind=kOutput, calls=%fused_computation.17 | convolution fusion | flops 1091305472 | bytes 4194304 | tf_op jit(solution)/shard_map/dot_general | solution.py:93
  440.7 9.6 %all-to-all-start = ((s32[32,1,8]{2,1,0:T(1,128)}), s32[32,1,8]{2,1,0:T(1,128)S(1)}, u32[]{:S(2)}, u32[]{:S(2)}) async-start(s32[32,1,8]{2,1,0:T(1,128)} %bitcast.21), calls=%async_computation.2 | async-start | bytes 32768 | tf_op jit(solution)/shard_map/all_to_all | solution.py:128
  450.3 62.5 %all-gather = bf16[256,4,128]{2,1,0:T(4,128)(2,1)S(1)} all-gather(bf16[1,4,128]{2,1,0:T(4,128)(2,1)S(1)} %bitcast.96), channel_id=1, replica_groups=mesh['dp'=32,'mp'=8] {'dp','mp'}, dimensions={0}, use_global_device_ids=true | all-gather | bytes 263168 | tf_op jit(solution)/shard_map/all_gather | solution.py:101
  517.2 1.7 broadcast_in_dim.14
  518.8 13.7 %scatter_fusion = bf16[256,32,128]{2,1,0:T(8,128)(2,1)} fusion(bf16[256,32,128]{2,1,0:T(8,128)(2,1)} %broadcast_in_dim.14, s32[128]{0:T(128)S(1)} %fusion.75, bf16[128,32,128]{2,1,0:T(8,128)(2,1)S(1)} %gather_fusion.2), kind=kCustom, calls=%fused_computation.6 | custom fusion | bytes 3146240 | tf_op jit(solution)/shard_map/scatter | solution.py:125
  532.5 6.3 %all-to-all-start.1 = ((bf16[32,8,32,128]{3,2,1,0:T(8,128)(2,1)}), bf16[32,8,32,128]{3,2,1,0:T(8,128)(2,1)S(1)}, u32[]{:S(2)}, u32[]{:S(2)}) async-start(bf16[32,8,32,128]{3,2,1,0:T(8,128)(2,1)} %bitcast.24), calls=%async_computation.3 | async-start | bytes 4194304 | tf_op jit(solution)/shard_map/all_to_all | solution.py:133
  538.9 11.8 %gather_fusion.3 = bf16[256,128,128]{2,1,0:T(8,128)(2,1)} fusion(bf16[256,128,128]{2,1,0:T(8,128)(2,1)} %param.24, s32[1024]{0:T(1024)S(1)} %pad_clamp_fusion.2), kind=kCustom, calls=%fused_computation.3 | custom fusion | bytes 16778240 | tf_op jit(solution)/shard_map/gather | solution.py:129
  550.8 1.9 gather_fusion.1
  552.9 34.5 %all-to-all-done.1 = bf16[32,8,32,128]{3,2,1,0:T(8,128)(2,1)S(1)} async-done(((bf16[32,8,32,128]{3,2,1,0:T(8,128)(2,1)}), bf16[32,8,32,128]{3,2,1,0:T(8,128)(2,1)S(1)}, u32[]{:S(2)}, u32[]{:S(2)}) %all-to-all-start.1) | async-done | bytes 2097184 | tf_op jit(solution)/shard_map/all_to_all | solution.py:133
  587.4 8.0 %select_reduce_fusion = bf16[32,8,32]{2,1,0:T(8,128)(2,1)S(1)} fusion(bf16[32,8,32,128]{3,2,1,0:T(8,128)(2,1)S(1)} %all-to-all-done.1, bf16[32,8,128,128]{3,2,1,0:T(8,128)(2,1)} %bitcast.87, pred[32,8,128]{2,1,0:T(8,128)(4,1)S(1)} %iota_compare_fusion.1), kind=kOutput, calls=%fused_computation.8 | convolution fusion | flops 270524416 | bytes 10534912 | tf_op jit(solution)/shard_map/snie,snte->snit/dot_general | solution.py:131
  596.0 7.8 %all-to-all-start.2 = ((bf16[32,2,128]{2,1,0:T(2,128)(2,1)}), bf16[32,2,128]{2,1,0:T(2,128)(2,1)S(1)}, u32[]{:S(2)}, u32[]{:S(2)}) async-start(bf16[32,2,128]{2,1,0:T(2,128)(2,1)} %reshape.374), calls=%async_computation.4 | async-start | bytes 32768 | tf_op jit(solution)/shard_map/all_to_all | solution.py:21
  603.8 8.6 %all-to-all-done.2 = bf16[32,2,128]{2,1,0:T(2,128)(2,1)S(1)} async-done(((bf16[32,2,128]{2,1,0:T(2,128)(2,1)}), bf16[32,2,128]{2,1,0:T(2,128)(2,1)S(1)}, u32[]{:S(2)}, u32[]{:S(2)}) %all-to-all-start.2) | async-done | bytes 16416 | tf_op jit(solution)/shard_map/all_to_all | solution.py:21
  (92 shorter events, 23.5 us)
Async XLA Ops:
  7.2 430.2 %copy-start = (s32[8192]{0:T(1024)S(1)}, s32[8192]{0:T(1024)}, u32[]{:S(2)}) copy-start(s32[8192]{0:T(1024)} %param.26) | copy-start | bytes 98308
  7.2 153.8 %all-gather.7.cloned.1.call-start = ((), (), s32[]{:S(2)}) async-start(), calls=%async_computation.5 | async-start | bytes 1179648 | tf_op jit(solution)/shard_map/all_gather | solution.py:45
  7.9 157.4 %all-gather.9.cloned.1.call-start = ((), (), s32[]{:S(2)}) async-start(), calls=%async_computation.6 | async-start | bytes 1081344 | tf_op jit(solution)/shard_map/all_gather | solution.py:48
  8.7 240.6 %reduce-scatter.3.cloned.1.call-start = ((), (), s32[]{:S(2)}) async-start(), calls=%async_computation.7 | async-start | bytes 1179648 | tf_op jit(solution)/shard_map/reduce_scatter | solution.py:85
  161.0 3.7 copy-start.3
  165.2 2.4 copy-start.7
  167.5 1.7 copy-start.4
  172.6 76.6 %copy-start.5 = (bf16[2,32,1024]{2,1,0:T(8,128)(2,1)S(1)}, bf16[2,32,1024]{2,1,0:T(8,128)(2,1)}, u32[]{:S(2)}) copy-start(bf16[2,32,1024]{2,1,0:T(8,128)(2,1)} %param.14) | copy-start | bytes 393220
  174.5 149.6 %all-gather.13.cloned.1.call-start = ((), (), s32[]{:S(2)}) async-start(), calls=%async_computation.9 | async-start | bytes 1081344 | tf_op jit(solution)/shard_map/all_gather | solution.py:91
  175.1 225.4 %all-gather.15.cloned.1.call-start = ((), (), s32[]{:S(2)}) async-start(), calls=%async_computation.10 | async-start | bytes 1081344 | tf_op jit(solution)/shard_map/all_gather | solution.py:94
  175.7 255.2 %all-gather.11.cloned.1.call-start = ((), (), s32[]{:S(2)}) async-start(), calls=%async_computation.8 | async-start | bytes 1179648 | tf_op jit(solution)/shard_map/all_gather | solution.py:90
  253.1 184.0 %copy-start.8 = (s32[2,16,4]{1,2,0:T(4,128)S(1)}, s32[2,16,4]{1,2,0:T(4,128)}, u32[]{:S(2)}) copy-start(s32[2,16,4]{1,2,0:T(4,128)} %param.27) | copy-start | bytes 1540
  253.1 197.2 %copy-start.9 = (bf16[4,128]{1,0:T(4,128)(2,1)S(1)}, bf16[4,128]{1,0:T(4,128)(2,1)}, u32[]{:S(2)}) copy-start(bf16[4,128]{1,0:T(4,128)(2,1)} %param.23) | copy-start | bytes 3076
  253.1 259.7 %reduce-scatter.5.cloned.1.call-start = ((), (), s32[]{:S(2)}) async-start(), calls=%async_computation.11 | async-start | bytes 1179648 | tf_op jit(solution)/shard_map/reduce_scatter | solution.py:96
  437.1 75.7 %copy-start.6 = (bf16[64,1024]{1,0:T(8,128)(2,1)S(1)}, bf16[64,1024]{1,0:T(8,128)(2,1)}, u32[]{:S(2)}) copy-start(bf16[64,1024]{1,0:T(8,128)(2,1)} %divide_convert_fusion.3) | copy-start | bytes 393220
  440.7 91.9 %all-to-all-start = ((s32[32,1,8]{2,1,0:T(1,128)}), s32[32,1,8]{2,1,0:T(1,128)S(1)}, u32[]{:S(2)}, u32[]{:S(2)}) async-start(s32[32,1,8]{2,1,0:T(1,128)} %bitcast.21), calls=%async_computation.2 | async-start | bytes 32768 | tf_op jit(solution)/shard_map/all_to_all | solution.py:128
  516.4 2.5 copy-start.2
  532.5 54.9 %all-to-all-start.1 = ((bf16[32,8,32,128]{3,2,1,0:T(8,128)(2,1)}), bf16[32,8,32,128]{3,2,1,0:T(8,128)(2,1)S(1)}, u32[]{:S(2)}, u32[]{:S(2)}) async-start(bf16[32,8,32,128]{3,2,1,0:T(8,128)(2,1)} %bitcast.24), calls=%async_computation.3 | async-start | bytes 4194304 | tf_op jit(solution)/shard_map/all_to_all | solution.py:133
  538.9 11.8 %copy-start.1 = (s32[256]{0:T(256)S(1)}, s32[256]{0:T(256)}, u32[]{:S(2)}) copy-start(s32[256]{0:T(256)} %param.25) | copy-start | bytes 3076
  596.0 16.4 %all-to-all-start.2 = ((bf16[32,2,128]{2,1,0:T(2,128)(2,1)}), bf16[32,2,128]{2,1,0:T(2,128)(2,1)S(1)}, u32[]{:S(2)}, u32[]{:S(2)}) async-start(bf16[32,2,128]{2,1,0:T(2,128)(2,1)} %reshape.374), calls=%async_computation.4 | async-start | bytes 32768 | tf_op jit(solution)/shard_map/all_to_all | solution.py:21
Sparse Core Ops, SparseCore 0:
  9.8 29.9 all-gather.6
  42.4 71.3 all-gather.8
  174.6 74.5 reduce-scatter.2
  251.7 72.3 all-gather.12
  326.6 73.8 all-gather.14
  402.1 28.6 all-gather.10
  437.2 32.1 reduce-scatter.4
where the time goes:
time: 622 us; the launch traced here: 621 us
  waiting for transfers between devices  297 us (48%)
  blocking collectives  215 us (35%)
  local copies, waits for them, and re-layouts  35.7 us (6%)
  matrix products  27.4 us (4%)
  starting transfers between devices  24 us (4%)
  between operations  14.6 us (2%)
  other arithmetic  7.57 us (1%)
    all_gather x1, waiting for transfers between devices, body(): lax.all_gather(w_down, 'dp', axis=1, tiled=True)  76.3 us
    reduce_scatter x1, waiting for transfers between devices, body(): lax.psum_scatter(attn_terms.astype(jnp.bfloat16), 'mp', scatter_dimension...  73.5 us
    all_gather x1, waiting for transfers between devices, body(): up = add_rows(mid_all, lax.all_gather(w_up, 'dp', axis=0, tiled=True))  70.8 us
    all_gather x1, blocking collectives, body(): lax.all_gather(w_proj, ('dp', 'mp'), axis=0, tiled=True)  62.5 us
    all_gather x1, blocking collectives, body(): lax.all_gather(query_weight, 'dp', axis=0, tiled=True)  41.4 us
    all_gather x1, blocking collectives, body(): lax.all_gather(w_key, 'dp', axis=0, tiled=True)  38.1 us
    all_gather x1, blocking collectives, body(): lax.all_gather(w_value, 'dp', axis=0, tiled=True)  37.2 us
    all_gather x1, blocking collectives, body(): lax.all_gather(w_out, 'dp', axis=1, tiled=True)  35.7 us
  transfers between devices with their start and end apart: 10, of which 6 were waited for; matrix products, arithmetic and copies ran while one was open for 7% of the time, Pallas kernels for 0%

commit v1 on v0

--- a/solution.py
+++ b/solution.py
@@ -48,7 +48,9 @@
     left_rel = lax.all_gather(rel_table, "dp", axis=0, tiled=True)
     pieces = (
         lax.all_gather(query_weight, "dp", axis=0, tiled=True),
-        lax.all_gather(w_key, "dp", axis=0, tiled=True),
+        jnp.concatenate(
+            lax.all_to_all(jnp.stack([w_key] * lax.axis_size("dp")), "dp", 0, 0), axis=0
+        ),
         lax.all_gather(w_value, "dp", axis=0, tiled=True),
     )
     qsum = add_rows(flat, pieces[0])

time: 622 us -> 588 us (0.945)
  blocking collectives: 215 us -> 177 us
  starting transfers between devices: 24 us -> 36.1 us
  waiting for transfers between devices: 297 us -> 286 us
    all_gather x1 -> x0, blocking collectives: 38.1 us -> none  [body(): lax.all_gather(w_key, 'dp', axis=0, tiled=True)]
    all_to_all x0 -> x1, starting transfers between devices: none -> 12 us  [body(): lax.all_to_all(jnp.stack([w_key] * lax.axis_size('dp')), 'dp', 0, 0)]
    reduce_scatter x1, waiting for transfers between devices: 73.5 us -> 62.7 us  [body(): lax.psum_scatter(attn_terms.astype(jnp.bfloat16), 'mp', scatter_dimension...]
  transfers between devices with their start and end apart: 10 -> 11, of which waited for: 6 -> 6; matrix products, arithmetic and copies ran while one was open for 7% -> 8% of each run, Pallas kernels for 0% -> 0%
where the time goes in v1:
time: 588 us; the launch traced here: 586 us
  waiting for transfers between devices  286 us (49%)
  blocking collectives  177 us (30%)
  local copies, waits for them, and re-layouts  37.9 us (6%)
  starting transfers between devices  36.1 us (6%)
  matrix products  27.4 us (5%)
  between operations  14.6 us (2%)
  other arithmetic  7.57 us (1%)
    all_gather x1, waiting for transfers between devices, body(): lax.all_gather(w_down, 'dp', axis=1, tiled=True)  76.3 us
    all_gather x1, waiting for transfers between devices, body(): up = add_rows(mid_all, lax.all_gather(w_up, 'dp', axis=0, tiled=True))  70.8 us
    reduce_scatter x1, waiting for transfers between devices, body(): lax.psum_scatter(attn_terms.astype(jnp.bfloat16), 'mp', scatter_dimension...  62.7 us
    all_gather x1, blocking collectives, body(): lax.all_gather(w_proj, ('dp', 'mp'), axis=0, tiled=True)  62.5 us
    all_gather x1, blocking collectives, body(): lax.all_gather(query_weight, 'dp', axis=0, tiled=True)  39.9 us
    all_gather x1, blocking collectives, body(): lax.all_gather(w_value, 'dp', axis=0, tiled=True)  38.7 us
    all_gather x1, blocking collectives, body(): lax.all_gather(w_out, 'dp', axis=1, tiled=True)  35.8 us
    all_to_all x1, waiting for transfers between devices, body(): lax.all_to_all(rows_out, 'dp', split_axis=0, concat_axis=0, tiled=True)  34.5 us
  transfers between devices with their start and end apart: 11, of which 6 were waited for; matrix products, arithmetic and copies ran while one was open for 8% of the time, Pallas kernels for 0%

profile of v1, /device:TPU:1, one launch (start us, length us, event | category | flops | bytes accessed | tf_op | source)
XLA Modules:
  0.0 586.3 jit_solution(3445798962036728554)
XLA Ops:
  10.1 12.0 %all-to-all-start = ((bf16[32,32,128]{2,1,0:T(8,128)(2,1)}), bf16[32,32,128]{2,1,0:T(8,128)(2,1)S(1)}, u32[]{:S(2)}, u32[]{:S(2)}) async-start(bf16[32,32,128]{2,1,0:T(8,128)(2,1)} %stack.2), calls=%async_computation | async-start | bytes 524288 | tf_op jit(solution)/shard_map/all_to_all | solution.py:52
  22.2 39.9 %all_gather.29 = bf16[1024,128]{1,0:T(8,128)(2,1)S(1)} all-gather(bf16[32,128]{1,0:T(8,128)(2,1)} %param.15), channel_id=1, replica_groups=mesh['dp'=32,'mp'=8] {'dp'}, dimensions={0}, use_global_device_ids=true | all-gather | bytes 270336 | tf_op jit(solution)/shard_map/all_gather | solution.py:50
  62.1 38.7 %all_gather.28 = bf16[1024,128]{1,0:T(8,128)(2,1)S(1)} all-gather(bf16[32,128]{1,0:T(8,128)(2,1)} %param.17), channel_id=1, replica_groups=mesh['dp'=32,'mp'=8] {'dp'}, dimensions={0}, use_global_device_ids=true | all-gather | bytes 270336 | tf_op jit(solution)/shard_map/all_gather | solution.py:54
  100.7 35.8 %all_gather.31 = bf16[128,1024]{0,1:T(8,128)(2,1)S(1)} all-gather(bf16[128,32]{0,1:T(8,128)(2,1)} %param.20), channel_id=1, replica_groups=mesh['dp'=32,'mp'=8] {'dp'}, dimensions={1}, use_global_device_ids=true | all-gather | bytes 270336 | tf_op jit(solution)/shard_map/all_gather | solution.py:84
  136.6 1.7 convolution_convert_fusion.6
  138.5 1.7 convolution_convert_fusion.5
  141.6 1.7 convolution_convert_fusion.4
  152.0 62.7 %reduce-scatter.3.cloned.1.call-done = bf16[64,1024]{1,0:T(8,128)(2,1)} async-done(((bf16[512,1024]{1,0:T(8,128)(2,1)}), bf16[64,1024]{1,0:T(8,128)(2,1)}) %reduce-scatter.3.cloned.1.call-update) | async-done | bytes 131088 | tf_op jit(solution)/shard_map/reduce_scatter | solution.py:87
  216.9 1.7 divide_convert_fusion.3
  218.8 70.8 %all-gather.13.cloned.1.call-done = bf16[1024,512]{1,0:T(8,128)(2,1)} async-done(((bf16[32,512]{1,0:T(8,128)(2,1)}), bf16[1024,512]{1,0:T(8,128)(2,1)}) %all-gather.13.cloned.1.call-update) | async-done | bytes 1048592 | tf_op jit(solution)/shard_map/all_gather | solution.py:93
  289.6 76.3 %all-gather.15.cloned.1.call-done = bf16[512,1024]{0,1:T(8,128)(2,1)} async-done(((bf16[512,32]{0,1:T(8,128)(2,1)}), bf16[512,1024]{0,1:T(8,128)(2,1)}) %all-gather.15.cloned.1.call-update) | async-done | bytes 1048592 | tf_op jit(solution)/shard_map/all_gather | solution.py:96
  365.9 30.5 %all-gather.11.cloned.1.call-done = bf16[512,1024]{1,0:T(8,128)(2,1)} async-done(((bf16[64,1024]{1,0:T(8,128)(2,1)}), bf16[512,1024]{1,0:T(8,128)(2,1)}) %all-gather.11.cloned.1.call-update) | async-done | bytes 1048592 | tf_op jit(solution)/shard_map/all_gather | solution.py:92
  396.4 6.2 %convolution_convert_fusion.1 = bf16[512,1024]{1,0:T(8,128)(2,1)} fusion(bf16[512,1024]{0,1:T(8,128)(2,1)} %all-gather.15.cloned.1.call-done, bf16[512,1024]{1,0:T(8,128)(2,1)} %all-gather.11.cloned.1.call-done, bf16[1024,512]{1,0:T(8,128)(2,1)} %all-gather.13.cloned.1.call-done), kind=kOutput, calls=%fused_computation.17 | convolution fusion | flops 1091305472 | bytes 4194304 | tf_op jit(solution)/shard_map/dot_general | solution.py:95
  406.2 9.6 %all-to-all-start.1 = ((s32[32,1,8]{2,1,0:T(1,128)}), s32[32,1,8]{2,1,0:T(1,128)S(1)}, u32[]{:S(2)}, u32[]{:S(2)}) async-start(s32[32,1,8]{2,1,0:T(1,128)} %bitcast.22), calls=%async_computation.3 | async-start | bytes 32768 | tf_op jit(solution)/shard_map/all_to_all | solution.py:130
  415.8 62.5 %all-gather = bf16[256,4,128]{2,1,0:T(4,128)(2,1)S(1)} all-gather(bf16[1,4,128]{2,1,0:T(4,128)(2,1)S(1)} %bitcast.99), channel_id=1, replica_groups=mesh['dp'=32,'mp'=8] {'dp','mp'}, dimensions={0}, use_global_device_ids=true | all-gather | bytes 263168 | tf_op jit(solution)/shard_map/all_gather | solution.py:103
  482.7 1.7 broadcast_in_dim.14
  484.3 13.7 %scatter_fusion = bf16[256,32,128]{2,1,0:T(8,128)(2,1)} fusion(bf16[256,32,128]{2,1,0:T(8,128)(2,1)} %broadcast_in_dim.14, s32[128]{0:T(128)S(1)} %fusion.75, bf16[128,32,128]{2,1,0:T(8,128)(2,1)S(1)} %gather_fusion.2), kind=kCustom, calls=%fused_computation.6 | custom fusion | bytes 3146240 | tf_op jit(solution)/shard_map/scatter | solution.py:127
  498.1 6.3 %all-to-all-start.2 = ((bf16[32,8,32,128]{3,2,1,0:T(8,128)(2,1)}), bf16[32,8,32,128]{3,2,1,0:T(8,128)(2,1)S(1)}, u32[]{:S(2)}, u32[]{:S(2)}) async-start(bf16[32,8,32,128]{3,2,1,0:T(8,128)(2,1)} %bitcast.25), calls=%async_computation.4 | async-start | bytes 4194304 | tf_op jit(solution)/shard_map/all_to_all | solution.py:135
  504.5 11.8 %gather_fusion.3 = bf16[256,128,128]{2,1,0:T(8,128)(2,1)} fusion(bf16[256,128,128]{2,1,0:T(8,128)(2,1)} %param.24, s32[1024]{0:T(1024)S(1)} %pad_clamp_fusion.2), kind=kCustom, calls=%fused_computation.3 | custom fusion | bytes 16778240 | tf_op jit(solution)/shard_map/gather | solution.py:131
  516.3 1.9 gather_fusion.1
  518.4 34.5 %all-to-all-done.2 = bf16[32,8,32,128]{3,2,1,0:T(8,128)(2,1)S(1)} async-done(((bf16[32,8,32,128]{3,2,1,0:T(8,128)(2,1)}), bf16[32,8,32,128]{3,2,1,0:T(8,128)(2,1)S(1)}, u32[]{:S(2)}, u32[]{:S(2)}) %all-to-all-start.2) | async-done | bytes 2097184 | tf_op jit(solution)/shard_map/all_to_all | solution.py:135
  552.9 8.0 %select_reduce_fusion = bf16[32,8,32]{2,1,0:T(8,128)(2,1)S(1)} fusion(bf16[32,8,32,128]{3,2,1,0:T(8,128)(2,1)S(1)} %all-to-all-done.2, bf16[32,8,128,128]{3,2,1,0:T(8,128)(2,1)} %bitcast.88, pred[32,8,128]{2,1,0:T(8,128)(4,1)S(1)} %iota_compare_fusion.1), kind=kOutput, calls=%fused_computation.8 | convolution fusion | flops 270524416 | bytes 10534912 | tf_op jit(solution)/shard_map/snie,snte->snit/dot_general | solution.py:133
  561.6 7.8 %all-to-all-start.3 = ((bf16[32,2,128]{2,1,0:T(2,128)(2,1)}), bf16[32,2,128]{2,1,0:T(2,128)(2,1)S(1)}, u32[]{:S(2)}, u32[]{:S(2)}) async-start(bf16[32,2,128]{2,1,0:T(2,128)(2,1)} %reshape.380), calls=%async_computation.5 | async-start | bytes 32768 | tf_op jit(solution)/shard_map/all_to_all | solution.py:21
  569.4 8.6 %all-to-all-done.3 = bf16[32,2,128]{2,1,0:T(2,128)(2,1)S(1)} async-done(((bf16[32,2,128]{2,1,0:T(2,128)(2,1)}), bf16[32,2,128]{2,1,0:T(2,128)(2,1)S(1)}, u32[]{:S(2)}, u32[]{:S(2)}) %all-to-all-start.3) | async-done | bytes 16416 | tf_op jit(solution)/shard_map/all_to_all | solution.py:21
  (96 shorter events, 25.7 us)
Async XLA Ops:
  7.2 395.7 %copy-start = (s32[8192]{0:T(1024)S(1)}, s32[8192]{0:T(1024)}, u32[]{:S(2)}) copy-start(s32[8192]{0:T(1024)} %param.26) | copy-start | bytes 98308
  7.2 129.4 %all-gather.7.cloned.1.call-start = ((), (), s32[]{:S(2)}) async-start(), calls=%async_computation.6 | async-start | bytes 1179648 | tf_op jit(solution)/shard_map/all_gather | solution.py:45
  7.9 133.7 %all-gather.9.cloned.1.call-start = ((), (), s32[]{:S(2)}) async-start(), calls=%async_computation.7 | async-start | bytes 1081344 | tf_op jit(solution)/shard_map/all_gather | solution.py:48
  10.1 128.4 %all-to-all-start = ((bf16[32,32,128]{2,1,0:T(8,128)(2,1)}), bf16[32,32,128]{2,1,0:T(8,128)(2,1)S(1)}, u32[]{:S(2)}, u32[]{:S(2)}) async-start(bf16[32,32,128]{2,1,0:T(8,128)(2,1)} %stack.2), calls=%async_computation | async-start | bytes 524288 | tf_op jit(solution)/shard_map/all_to_all | solution.py:52
  22.1 192.6 %reduce-scatter.3.cloned.1.call-start = ((), (), s32[]{:S(2)}) async-start(), calls=%async_computation.8 | async-start | bytes 1179648 | tf_op jit(solution)/shard_map/reduce_scatter | solution.py:87
  136.6 3.7 copy-start.3
  140.7 3.1 copy-start.8
  143.8 1.7 copy-start.4
  146.5 2.1 copy-start.7
  148.9 65.8 %copy-start.5 = (bf16[2,32,1024]{2,1,0:T(8,128)(2,1)S(1)}, bf16[2,32,1024]{2,1,0:T(8,128)(2,1)}, u32[]{:S(2)}) copy-start(bf16[2,32,1024]{2,1,0:T(8,128)(2,1)} %param.14) | copy-start | bytes 393220
  150.8 138.9 %all-gather.13.cloned.1.call-start = ((), (), s32[]{:S(2)}) async-start(), calls=%async_computation.10 | async-start | bytes 1081344 | tf_op jit(solution)/shard_map/all_gather | solution.py:93
  151.4 214.6 %all-gather.15.cloned.1.call-start = ((), (), s32[]{:S(2)}) async-start(), calls=%async_computation.11 | async-start | bytes 1081344 | tf_op jit(solution)/shard_map/all_gather | solution.py:96
  151.9 244.5 %all-gather.11.cloned.1.call-start = ((), (), s32[]{:S(2)}) async-start(), calls=%async_computation.9 | async-start | bytes 1179648 | tf_op jit(solution)/shard_map/all_gather | solution.py:92
  218.6 184.1 %copy-start.9 = (s32[2,16,4]{1,2,0:T(4,128)S(1)}, s32[2,16,4]{1,2,0:T(4,128)}, u32[]{:S(2)}) copy-start(s32[2,16,4]{1,2,0:T(4,128)} %param.27) | copy-start | bytes 1540
  218.6 197.2 %copy-start.10 = (bf16[4,128]{1,0:T(4,128)(2,1)S(1)}, bf16[4,128]{1,0:T(4,128)(2,1)}, u32[]{:S(2)}) copy-start(bf16[4,128]{1,0:T(4,128)(2,1)} %param.23) | copy-start | bytes 3076
  218.6 259.7 %reduce-scatter.5.cloned.1.call-start = ((), (), s32[]{:S(2)}) async-start(), calls=%async_computation.12 | async-start | bytes 1179648 | tf_op jit(solution)/shard_map/reduce_scatter | solution.py:98
  402.6 75.7 %copy-start.6 = (bf16[64,1024]{1,0:T(8,128)(2,1)S(1)}, bf16[64,1024]{1,0:T(8,128)(2,1)}, u32[]{:S(2)}) copy-start(bf16[64,1024]{1,0:T(8,128)(2,1)} %divide_convert_fusion.3) | copy-start | bytes 393220
  406.2 91.9 %all-to-all-start.1 = ((s32[32,1,8]{2,1,0:T(1,128)}), s32[32,1,8]{2,1,0:T(1,128)S(1)}, u32[]{:S(2)}, u32[]{:S(2)}) async-start(s32[32,1,8]{2,1,0:T(1,128)} %bitcast.22), calls=%async_computation.3 | async-start | bytes 32768 | tf_op jit(solution)/shard_map/all_to_all | solution.py:130
  481.9 2.5 copy-start.2
  498.1 54.9 %all-to-all-start.2 = ((bf16[32,8,32,128]{3,2,1,0:T(8,128)(2,1)}), bf16[32,8,32,128]{3,2,1,0:T(8,128)(2,1)S(1)}, u32[]{:S(2)}, u32[]{:S(2)}) async-start(bf16[32,8,32,128]{3,2,1,0:T(8,128)(2,1)} %bitcast.25), calls=%async_computation.4 | async-start | bytes 4194304 | tf_op jit(solution)/shard_map/all_to_all | solution.py:135
  504.4 11.8 %copy-start.1 = (s32[256]{0:T(256)S(1)}, s32[256]{0:T(256)}, u32[]{:S(2)}) copy-start(s32[256]{0:T(256)} %param.25) | copy-start | bytes 3076
  561.6 16.4 %all-to-all-start.3 = ((bf16[32,2,128]{2,1,0:T(2,128)(2,1)}), bf16[32,2,128]{2,1,0:T(2,128)(2,1)S(1)}, u32[]{:S(2)}, u32[]{:S(2)}) async-start(bf16[32,2,128]{2,1,0:T(2,128)(2,1)} %reshape.380), calls=%async_computation.5 | async-start | bytes 32768 | tf_op jit(solution)/shard_map/all_to_all | solution.py:21
Sparse Core Ops, SparseCore 0:
  9.8 29.9 all-gather.6
  42.4 71.3 all-gather.8
  150.9 63.7 reduce-scatter.2
  217.2 72.4 all-gather.12
  292.1 73.8 all-gather.14
  367.7 28.6 all-gather.10
  402.8 32.1 reduce-scatter.4
